TPU v7x, 32 devices: a whole 2x2x4 slice. The times are simulated.
32 devices in a mesh: groups: 2 (over x), seq: 8 (over z, y), samp: 2 (over core).
Axes of the slice: x: 2, y: 2, z: 4, core: 2. Of those that a mesh axis runs over, the one named last changes fastest.
Arguments:
- q_proj: bfloat16 [4, 2048, 4096], P(('groups', 'samp'), 'seq'), parts along dimension 0, may hold values from -750 to 750
- q_tangent: bfloat16 [4, 2048, 4096], P(('groups', 'samp'), 'seq'), parts along dimension 0, may hold values from -750 to 750
- k_proj: bfloat16 [4, 2048, 4096], P(('groups', 'samp'), 'seq'), parts along dimension 0, may hold values from -750 to 750
- k_tangent: bfloat16 [4, 2048, 4096], P(('groups', 'samp'), 'seq'), parts along dimension 0, may hold values from -750 to 750
- v_proj: bfloat16 [4, 2048, 4096], P(('groups', 'samp'), 'seq'), parts along dimension 0, may hold values from -6 to 6
- v_tangent: bfloat16 [4, 2048, 4096], P(('groups', 'samp'), 'seq'), parts along dimension 0, may hold values from -6 to 6
- query_norm_gain: float32 [4096], replicated, may hold values from 0.5 to 2
- key_norm_gain: float32 [4096], replicated, may hold values from 0.5 to 2
- lengths: int32 [4, 4], P('groups'), parts along dimension 0, may hold values from 1 to 768, 2048 in all within a row
Outputs:
- attended: float32 [4, 2048, 4096], P(('groups', 'samp'), 'seq'), parts along dimension 0
- attended_tangent: float32 [4, 2048, 4096], P(('groups', 'samp'), 'seq'), parts along dimension 0
There are 2 independent parts, one for each index of `groups`. A program takes and returns all parts, laid end to end along the dimension named above; an argument that names none is the same for every part. Nothing has to cross between parts.
Inputs may be any that keep to these rules, and one draw needn't show every extreme that they name: `lengths`: each row sums to 2048 and its largest entry is 768.
All inputs are finite; a program needn't handle non-finite values.
Results may differ from a plain program's by a relative error of at most 0.022.
The roundings to bfloat16 on the way count: a program that leaves them out, or rounds other values in their place, can miss the bound.
Values may be sent and summed in bfloat16 or wider, within the bound.
No kernel may reach another device: no remote copies, remote signals or barrier semaphores. Data moves between devices by JAX's collectives and lax.ppermute only.
A program may use at most 128 MiB of HBM per device.

v0:
```python
import math

import jax
import jax.numpy as jnp
from jax import lax
from jax.experimental import pallas as pl
from jax.experimental.pallas import tpu as pltpu
from jax.sharding import PartitionSpec as P


HEAD_DIM = 128
BLOCK = 256
KEY_BLOCK = 256


def normalize(source, source_tangent, gain):
    widened = source.astype(jnp.float32)
    dwidened = source_tangent.astype(jnp.float32)
    inverse = lax.rsqrt(jnp.mean(widened * widened, axis=-1, keepdims=True) + 1e-06)
    radial = jnp.mean(widened * dwidened, axis=-1, keepdims=True)
    normed = (widened * inverse * gain).astype(jnp.bfloat16)
    tangent = ((dwidened * inverse - widened * inverse**3 * radial) * gain).astype(jnp.bfloat16)
    return (normed, tangent)


def block_tables(sample_lengths, count):
    sample_ends = jnp.cumsum(sample_lengths).astype(jnp.int32)
    sample_starts = sample_ends - sample_lengths
    blocks = count // BLOCK
    first_rows = jnp.arange(blocks, dtype=jnp.int32) * BLOCK
    last_rows = first_rows + (BLOCK - 1)
    first_segment = jnp.sum((first_rows[:, None] >= sample_ends[None, :]).astype(jnp.int32), axis=1)
    last_segment = jnp.sum((last_rows[:, None] >= sample_ends[None, :]).astype(jnp.int32), axis=1)
    samples = sample_lengths.shape[0]
    first_segment = jnp.clip(first_segment, 0, samples - 1)
    last_segment = jnp.clip(last_segment, 0, samples - 1)
    first_key = jnp.take(sample_starts, first_segment)
    last_key = jnp.take(sample_ends, last_segment)
    key_blocks = count // KEY_BLOCK
    first_block = jnp.clip(first_key // KEY_BLOCK, 0, key_blocks - 1)
    last_block = jnp.clip((last_key - 1) // KEY_BLOCK + 1, first_block + 1, key_blocks)
    return first_block.astype(jnp.int32), last_block.astype(jnp.int32), sample_ends


def attention_kernel(
    first_ref, last_ref, ends_ref,
    q_ref, dq_ref, k_ref, dk_ref, v_ref, dv_ref,
    result_ref,
):
    i = pl.program_id(1)
    samples = ends_ref.shape[0]
    factor = 1.0 / math.sqrt(HEAD_DIM)
    queries = q_ref[...]
    dqueries = dq_ref[...]
    both_queries = jnp.concatenate([dqueries, queries], axis=1)

    def segment_of(positions):
        seg = jnp.zeros(positions.shape, jnp.int32)
        for j in range(samples):
            seg = seg + (positions >= ends_ref[j]).astype(jnp.int32)
        return seg

    query_positions = i * BLOCK + lax.broadcasted_iota(jnp.int32, (BLOCK, 1), 0)
    query_segment = segment_of(query_positions)
    first = first_ref[i]
    last = last_ref[i]

    def scores_of(kb):
        start = kb * KEY_BLOCK
        key_rows = k_ref[kb]
        key_positions = start + lax.broadcasted_iota(jnp.int32, (1, KEY_BLOCK), 1)
        same = query_segment == segment_of(key_positions)
        raw = lax.dot_general(
            queries, key_rows, (((1,), (1,)), ((), ())), preferred_element_type=jnp.float32
        ) * factor
        return raw, same, start, key_rows

    def statistics(kb, carry):
        row_top, total = carry
        raw, same, _, _ = scores_of(kb)
        masked = jnp.where(same, raw, -1e30)
        new_top = jnp.maximum(row_top, jnp.max(masked, axis=1, keepdims=True))
        exponent = jnp.where(same, jnp.exp(masked - new_top), 0.0)
        total = total * jnp.exp(row_top - new_top) + jnp.sum(exponent, axis=1, keepdims=True)
        return new_top, total

    row_top, total = lax.fori_loop(
        first, last, statistics,
        (jnp.full((BLOCK, 1), -1e30, jnp.float32), jnp.zeros((BLOCK, 1), jnp.float32)),
    )
    inverse_total = 1.0 / total

    def sums(kb, carry):
        center, output, spread_sum, dvalue_sum = carry
        raw, same, _, key_rows = scores_of(kb)
        dkey_rows = dk_ref[kb]
        value_rows = v_ref[kb]
        dvalue_rows = dv_ref[kb]
        both_keys = jnp.concatenate([key_rows, dkey_rows], axis=1)
        dscores = lax.dot_general(
            both_queries, both_keys, (((1,), (1,)), ((), ())), preferred_element_type=jnp.float32
        ) * factor
        weights = jnp.where(same, jnp.exp(raw - row_top), 0.0) * inverse_total
        product = jnp.where(same, weights * dscores, 0.0)
        center = center + jnp.sum(product, axis=1, keepdims=True)
        rounded = weights.astype(jnp.bfloat16)
        spread = product.astype(jnp.bfloat16)
        output = output + jnp.dot(rounded, value_rows, preferred_element_type=jnp.float32)
        spread_sum = spread_sum + jnp.dot(spread, value_rows, preferred_element_type=jnp.float32)
        dvalue_sum = dvalue_sum + jnp.dot(rounded, dvalue_rows, preferred_element_type=jnp.float32)
        return center, output, spread_sum, dvalue_sum

    empty = jnp.zeros((BLOCK, HEAD_DIM), jnp.float32)
    center, output, spread_sum, dvalue_sum = lax.fori_loop(
        first, last, sums, (jnp.zeros((BLOCK, 1), jnp.float32), empty, empty, empty)
    )
    result_ref[0] = output.astype(result_ref.dtype)
    result_ref[1] = (spread_sum - center * output + dvalue_sum).astype(result_ref.dtype)


def attend(stacked, values, heads, offset, first_block, last_block, sample_ends, result_dtype):
    sources = stacked.shape[0]
    all_heads = values.shape[1] // 2

    def query_spec(t):
        return pl.BlockSpec((None, None, BLOCK, HEAD_DIM), lambda h, i, *_: (i, t * heads + h, 0, 0))

    def key_spec(t):
        return pl.BlockSpec((sources, None, BLOCK, HEAD_DIM), lambda h, i, *_: (0, t * heads + h, 0, 0))

    def value_spec(t):
        return pl.BlockSpec(
            (sources, None, BLOCK, HEAD_DIM), lambda h, i, *_: (0, t * all_heads + offset + h, 0, 0)
        )

    grid_spec = pltpu.PrefetchScalarGridSpec(
        num_scalar_prefetch=3,
        grid=(heads, sources),
        in_specs=[query_spec(0), query_spec(1), key_spec(2), key_spec(3), value_spec(0), value_spec(1)],
        out_specs=pl.BlockSpec((None, 2, BLOCK, HEAD_DIM), lambda h, i, *_: (i, 0, 0, h)),
    )
    return pl.pallas_call(
        attention_kernel,
        grid_spec=grid_spec,
        out_shape=jax.ShapeDtypeStruct((sources, 2, BLOCK, heads * HEAD_DIM), result_dtype),
        compiler_params=pltpu.CompilerParams(
            dimension_semantics=("arbitrary", "arbitrary"),
        ),
    )(first_block, last_block, sample_ends, stacked, stacked, stacked, stacked, values, values)


def gather_kernel(*refs):
    *sources, out_ref = refs
    per_step = out_ref.shape[0]
    heads = out_ref.shape[1] // len(sources)
    for d in range(per_step):
        for t, ref in enumerate(sources):
            for h in range(heads):
                column = (d * heads + h) * HEAD_DIM
                out_ref[d, t * heads + h] = ref[:, column:column + HEAD_DIM]


GATHER_STEPS = 2


def by_destination_all(arrays, destinations):
    tokens, width = arrays[0].shape[1], arrays[0].shape[2]
    local_width = width // destinations
    heads = local_width // HEAD_DIM
    steps = GATHER_STEPS if destinations % GATHER_STEPS == 0 else 1
    per_step = destinations // steps
    in_spec = pl.BlockSpec((None, tokens, per_step * local_width), lambda d: (0, 0, d))
    return pl.pallas_call(
        gather_kernel,
        grid=(steps,),
        in_specs=[in_spec] * len(arrays),
        out_specs=pl.BlockSpec(
            (per_step, len(arrays) * heads, tokens, HEAD_DIM), lambda d: (d, 0, 0, 0)
        ),
        out_shape=jax.ShapeDtypeStruct(
            (destinations, len(arrays) * heads, tokens, HEAD_DIM), arrays[0].dtype
        ),
    )(*arrays)


def assemble_kernel(*refs):
    *received, out_ref, tan_ref = refs
    per_step = received[0].shape[0]
    local_width = out_ref.shape[1] // per_step
    for s in range(per_step):
        offset = s * local_width
        for r in received:
            w = r.shape[-1]
            out_ref[:, offset:offset + w] = r[s, 0].astype(jnp.float32)
            tan_ref[:, offset:offset + w] = r[s, 1].astype(jnp.float32)
            offset += w


ASSEMBLE_STEPS = 2


def assemble(received, tokens, width):
    sources = received[0].shape[0]
    local_width = width // sources
    steps = ASSEMBLE_STEPS if sources % ASSEMBLE_STEPS == 0 else 1
    per_step = sources // steps
    in_specs = [
        pl.BlockSpec((per_step, 2, tokens, r.shape[3]), lambda s: (s, 0, 0, 0)) for r in received
    ]
    out_spec = pl.BlockSpec((None, tokens, per_step * local_width), lambda s: (0, 0, s))
    return pl.pallas_call(
        assemble_kernel,
        grid=(steps,),
        in_specs=in_specs,
        out_specs=[out_spec, out_spec],
        out_shape=[
            jax.ShapeDtypeStruct((1, tokens, width), jnp.float32),
            jax.ShapeDtypeStruct((1, tokens, width), jnp.float32),
        ],
    )(*received)


def chunk_sizes(local_heads):
    if local_heads <= 2:
        return [1] * local_heads
    return [1, 1, local_heads - 2]


RESULT_DTYPE = jnp.bfloat16


def per_device_body(
    q_proj, q_tangent, k_proj, k_tangent, v_proj, v_tangent, query_norm_gain, key_norm_gain, lengths
):
    seq_count = lax.axis_size("seq")
    tokens = q_proj.shape[1]
    width = q_proj.shape[2]
    local_heads = width // HEAD_DIM // seq_count
    pack_tokens = tokens * seq_count
    sizes = chunk_sizes(local_heads)
    starts = [sum(sizes[:c]) for c in range(len(sizes))]

    assert tokens == BLOCK

    def by_destination(array, heads):
        split = array.reshape(tokens, seq_count, local_heads, HEAD_DIM)[:, :, heads]
        return jnp.transpose(split, (1, 2, 0, 3))

    value_payload = by_destination_all((v_proj, v_tangent), seq_count)
    values = lax.all_to_all(value_payload, "seq", split_axis=0, concat_axis=0, tiled=True)

    q_normed, dq_normed = normalize(q_proj, q_tangent, query_norm_gain)
    k_normed, dk_normed = normalize(k_proj, k_tangent, key_norm_gain)
    own_row = lax.dynamic_slice_in_dim(lengths, lax.axis_index("samp"), 1, 0)[0]
    first_block, last_block, sample_ends = block_tables(own_row, pack_tokens)
    normed = (q_normed, dq_normed, k_normed, dk_normed)
    results = []
    for first_head, chunk_heads in zip(starts, sizes):
        heads = slice(first_head, first_head + chunk_heads)
        payload = jnp.concatenate([by_destination(array, heads) for array in normed], axis=1)
        stacked = lax.all_to_all(payload, "seq", split_axis=0, concat_axis=0, tiled=True)
        result = attend(
            stacked, values, chunk_heads, first_head,
            first_block, last_block, sample_ends, RESULT_DTYPE,
        )
        results.append(result)
    received = []
    for members in (results[:2], results[2:]):
        if not members:
            continue
        group = jnp.concatenate(members, axis=3)
        received.append(lax.all_to_all(group, "seq", split_axis=0, concat_axis=0, tiled=True))
    return tuple(assemble(received, tokens, width))


def solution(mesh):
    placed = (
        P(("groups", "samp"), "seq", None),
        P(("groups", "samp"), "seq", None),
        P(("groups", "samp"), "seq", None),
        P(("groups", "samp"), "seq", None),
        P(("groups", "samp"), "seq", None),
        P(("groups", "samp"), "seq", None),
        P(),
        P(),
        P("groups", None),
    )
    return jax.shard_map(
        per_device_body,
        mesh=mesh,
        in_specs=placed,
        out_specs=(P(("groups", "samp"), "seq", None), P(("groups", "samp"), "seq", None)),
        check_vma=False,
    )
```

profile of v0, /device:TPU:0, one launch (start us, length us, event | category | flops | bytes accessed | tf_op | source)
XLA Modules:
  0.0 456.9 jit_solution(2666554955021308007)
XLA Ops:
  0.6 3.3 copy.27
  3.9 4.1 copy.29
  8.0 2.6 fusion.6
  10.7 2.4 fusion.8
  16.4 2.1 copy.43
  18.5 3.3 copy.31
  21.7 4.1 copy.33
  25.8 2.6 fusion.11
  28.5 2.4 fusion.13
  30.9 1.4 copy-done.10
  33.3 2.0 copy.46
  37.7 2.9 pad_maximum_fusion.1
  40.7 7.3 %all-to-all-start = ((bf16[8,4,256,128]{3,2,1,0:T(8,128)(2,1)}), bf16[8,4,256,128]{3,2,1,0:T(8,128)(2,1)S(1)}, u32[]{:S(2)}, u32[]{:S(2)}) async-start(bf16[8,4,256,128]{3,2,1,0:T(8,128)(2,1)} %pad_maximum_fusion.1), calls=%async_computation | async-start | bytes 4194304 | tf_op jit(solution)/shard_map/all_to_all | solution.py:261
  50.0 2.1 copy.50
  53.1 3.0 pad_maximum_fusion.2
  56.1 40.2 %all-to-all-done.q_ref.dq_ref.k_ref.dk_ref = bf16[8,4,256,128]{3,2,1,0:T(8,128)(2,1)S(1)} async-done(((bf16[8,4,256,128]{3,2,1,0:T(8,128)(2,1)}), bf16[8,4,256,128]{3,2,1,0:T(8,128)(2,1)S(1)}, u32[]{:S(2)}, u32[]{:S(2)}) %all-to-all-start) | async-done | bytes 2097184 | tf_op jit(solution)/shard_map/all_to_all | solution.py:261
  97.6 4.4 all-to-all-start.2
  102.0 3.9 shard_map.104
  105.9 43.9 %all-to-all-done.2.q_ref.dq_ref.k_ref.dk_ref = bf16[8,4,256,128]{3,2,1,0:T(8,128)(2,1)} async-done(((bf16[8,4,256,128]{3,2,1,0:T(8,128)(2,1)}), bf16[8,4,256,128]{3,2,1,0:T(8,128)(2,1)}, u32[]{:S(2)}, u32[]{:S(2)}) %all-to-all-start.2) | async-done | bytes 2097184 | tf_op jit(solution)/shard_map/all_to_all | solution.py:261
  149.8 4.6 all-to-all-start.1
  154.5 1.5 copy-done.5
  164.0 4.1 pad_maximum_fusion
  168.2 78.7 %all-to-all-done.1.v_ref.dv_ref = bf16[8,8,256,128]{3,2,1,0:T(8,128)(2,1)} async-done(((bf16[8,8,256,128]{3,2,1,0:T(8,128)(2,1)}), bf16[8,8,256,128]{3,2,1,0:T(8,128)(2,1)}, u32[]{:S(2)}, u32[]{:S(2)}) %all-to-all-start.1) | async-done | bytes 4194336 | tf_op jit(solution)/shard_map/all_to_all | solution.py:250
  246.9 4.7 %all-to-all-start.4 = ((bf16[8,8,256,128]{3,2,1,0:T(8,128)(2,1)}), bf16[8,8,256,128]{3,2,1,0:T(8,128)(2,1)}, u32[]{:S(2)}, u32[]{:S(2)}) async-start(bf16[8,8,256,128]{3,2,1,0:T(8,128)(2,1)} %pad_maximum_fusion), calls=%async_computation.4 | async-start | bytes 8388608 | tf_op jit(solution)/shard_map/all_to_all | solution.py:261
  253.8 26.2 %shard_map.106 = bf16[8,2,256,128]{3,2,1,0:T(8,128)(2,1)} custom-call(s32[8]{0:T(128)} %get-tuple-element.10.first_ref, s32[8]{0:T(128)} %get-tuple-element.9.last_ref, s32[4]{0:T(128)} %bitcast.24, bf16[8,4,256,128]{3,2,1,0:T(8,128)(2,1)} %all-to-all-done.2.q_ref.dq_ref.k_ref.dk_ref, bf16[8,4,256,128]{3,2,1,0:T(8,128)(2,1)} %all-to-all-done.2.q_ref.dq_ref.k_ref.dk_ref, ...), custom_call_target="tpu_custom_call" | custom-call | tf_op jit(solution)/shard_map/pallas_call | solution.py:142
  280.0 26.3 %shard_map.105 = bf16[8,2,256,128]{3,2,1,0:T(8,128)(2,1)} custom-call(s32[8]{0:T(128)} %get-tuple-element.10.first_ref, s32[8]{0:T(128)} %get-tuple-element.9.last_ref, s32[4]{0:T(128)} %bitcast.25, bf16[8,4,256,128]{3,2,1,0:T(8,128)(2,1)} %copy-done.1, bf16[8,4,256,128]{3,2,1,0:T(8,128)(2,1)} %copy-done.1, bf16[8,4,256,128]{3,2,1,0:T(8,128)(2,1)} %copy-done.1, ...), custom_call_target="tpu_custom_call" | custom-call | tf_op jit(solution)/shard_map/pallas_call | solution.py:142
  306.3 2.8 pad_maximum_fusion.3
  309.2 34.9 %all-to-all-done.4.q_ref.dq_ref.k_ref.dk_ref = bf16[8,8,256,128]{3,2,1,0:T(8,128)(2,1)} async-done(((bf16[8,8,256,128]{3,2,1,0:T(8,128)(2,1)}), bf16[8,8,256,128]{3,2,1,0:T(8,128)(2,1)}, u32[]{:S(2)}, u32[]{:S(2)}) %all-to-all-start.4) | async-done | bytes 4194336 | tf_op jit(solution)/shard_map/all_to_all | solution.py:261
  344.1 3.6 all-to-all-start.3
  347.7 50.1 %shard_map.107 = bf16[8,2,256,256]{3,2,1,0:T(8,128)(2,1)} custom-call(s32[8]{0:T(128)} %get-tuple-element.10.first_ref, s32[8]{0:T(128)} %get-tuple-element.9.last_ref, s32[4]{0:T(128)} %bitcast.26, bf16[8,8,256,128]{3,2,1,0:T(8,128)(2,1)} %all-to-all-done.4.q_ref.dq_ref.k_ref.dk_ref, bf16[8,8,256,128]{3,2,1,0:T(8,128)(2,1)} %all-to-all-done.4.q_ref.dq_ref.k_ref.dk_ref, ...), custom_call_target="tpu_custom_call" | custom-call | tf_op jit(solution)/shard_map/pallas_call | solution.py:142
  397.8 53.9 %all_to_all.30.refs_1_ = bf16[8,2,256,256]{3,2,1,0:T(8,128)(2,1)} all-to-all(bf16[8,2,256,256]{3,2,1,0:T(8,128)(2,1)} %shard_map.107), channel_id=1, replica_groups=mesh['groups'=2,'seq'=8,'samp'=2] {'seq'}, dimensions={0} | all-to-all | bytes 4194304 | tf_op jit(solution)/shard_map/all_to_all | solution.py:272
  451.7 5.1 %shard_map.108 = (f32[1,256,4096]{2,1,0:T(8,128)}, f32[1,256,4096]{2,1,0:T(8,128)}) custom-call(bf16[8,2,256,256]{3,2,1,0:T(8,128)(2,1)} %copy-done.12, bf16[8,2,256,256]{3,2,1,0:T(8,128)(2,1)} %all_to_all.30.refs_1_), custom_call_target="tpu_custom_call" | custom-call | tf_op jit(solution)/shard_map/pallas_call | solution.py:211
  (74 shorter events, 21.5 us)
Async XLA Ops:
  8.0 2.6 copy-start.2
  8.0 2.7 copy-start.19
  13.1 1.4 copy-start.6
  13.1 2.4 copy-start.4
  25.8 2.6 copy-start.3
  25.8 2.7 copy-start.20
  30.9 1.4 copy-start.10
  30.9 4.5 copy-start.8
  40.7 55.5 %all-to-all-start = ((bf16[8,4,256,128]{3,2,1,0:T(8,128)(2,1)}), bf16[8,4,256,128]{3,2,1,0:T(8,128)(2,1)S(1)}, u32[]{:S(2)}, u32[]{:S(2)}) async-start(bf16[8,4,256,128]{3,2,1,0:T(8,128)(2,1)} %pad_maximum_fusion.1), calls=%async_computation | async-start | bytes 4194304 | tf_op jit(solution)/shard_map/all_to_all | solution.py:261
  49.0 3.1 copy-start.17
  50.0 3.1 copy-start.18
  96.2 1.4 copy-start.1
  97.6 52.2 %all-to-all-start.2 = ((bf16[8,4,256,128]{3,2,1,0:T(8,128)(2,1)}), bf16[8,4,256,128]{3,2,1,0:T(8,128)(2,1)}, u32[]{:S(2)}, u32[]{:S(2)}) async-start(bf16[8,4,256,128]{3,2,1,0:T(8,128)(2,1)} %pad_maximum_fusion.2), calls=%async_computation.2 | async-start | bytes 4194304 | tf_op jit(solution)/shard_map/all_to_all | solution.py:261
  105.9 48.5 %copy-start.7 = (bf16[1,256,4096]{1,2,0:T(8,128)(2,1)S(1)}, bf16[1,256,4096]{1,2,0:T(8,128)(2,1)}, u32[]{:S(2)}) copy-start(bf16[1,256,4096]{1,2,0:T(8,128)(2,1)} %copy-done.6) | copy-start | bytes 6291460
  149.8 97.1 %all-to-all-start.1 = ((bf16[8,8,256,128]{3,2,1,0:T(8,128)(2,1)}), bf16[8,8,256,128]{3,2,1,0:T(8,128)(2,1)}, u32[]{:S(2)}, u32[]{:S(2)}) async-start(bf16[8,8,256,128]{3,2,1,0:T(8,128)(2,1)} %shard_map.104), calls=%async_computation.1 | async-start | bytes 8388608 | tf_op jit(solution)/shard_map/all_to_all | solution.py:250
  154.4 1.6 copy-start.5
  154.4 2.2 copy-start.11
  155.9 1.7 copy-start.9
  160.0 2.7 copy-start.13
  161.4 2.7 copy-start.14
  162.7 1.3 copy-start.15
  168.2 83.5 %copy-start.21 = (s32[2,4]{1,0:T(2,128)S(1)}, s32[2,4]{1,0:T(2,128)}, u32[]{:S(2)}) copy-start(s32[2,4]{1,0:T(2,128)} %param.19) | copy-start | bytes 100
  246.9 97.2 %all-to-all-start.4 = ((bf16[8,8,256,128]{3,2,1,0:T(8,128)(2,1)}), bf16[8,8,256,128]{3,2,1,0:T(8,128)(2,1)}, u32[]{:S(2)}, u32[]{:S(2)}) async-start(bf16[8,8,256,128]{3,2,1,0:T(8,128)(2,1)} %pad_maximum_fusion), calls=%async_computation.4 | async-start | bytes 8388608 | tf_op jit(solution)/shard_map/all_to_all | solution.py:261
  251.8 2.0 copy-start
  280.0 26.3 %copy-start.16 = (bf16[8,2,256,128]{3,2,1,0:T(8,128)(2,1)S(1)}, bf16[8,2,256,128]{3,2,1,0:T(8,128)(2,1)}, u32[]{:S(2)}) copy-start(bf16[8,2,256,128]{3,2,1,0:T(8,128)(2,1)} %shard_map.106) | copy-start | bytes 3145732
  344.1 53.8 %all-to-all-start.3 = ((bf16[8,2,256,256]{3,2,1,0:T(8,128)(2,1)}), bf16[8,2,256,256]{3,2,1,0:T(8,128)(2,1)S(1)}, u32[]{:S(2)}, u32[]{:S(2)}) async-start(bf16[8,2,256,256]{3,2,1,0:T(8,128)(2,1)} %pad_maximum_fusion.3), calls=%async_computation.3 | async-start | bytes 4194304 | tf_op jit(solution)/shard_map/all_to_all | solution.py:272
  397.8 53.9 %copy-start.12 = (bf16[8,2,256,256]{3,2,1,0:T(8,128)(2,1)}, bf16[8,2,256,256]{3,2,1,0:T(8,128)(2,1)S(1)}, u32[]{:S(2)}) copy-start(bf16[8,2,256,256]{3,2,1,0:T(8,128)(2,1)S(1)} %all-to-all-done.3.refs_0_) | copy-start | bytes 6291460
where the time goes:
time: 458 us; the launch traced here: 457 us
  waiting for transfers between devices  198 us (43%)
  Pallas kernels  112 us (24%)
  blocking collectives  53.9 us (12%)
  local copies, waits for them, and re-layouts  44.3 us (10%)
  starting transfers between devices  24.6 us (5%)
  other arithmetic  23.8 us (5%)
    all_to_all x3, waiting for transfers between devices, per_device_body(): lax.all_to_all(payload, 'seq', split_axis=0, concat_axis=0, tiled=True)  119 us
    pallas_call x3, Pallas kernels, attend(): pl.pallas_call(attention_kernel, grid_spec=grid_spec, out_shape=jax.Shape...  103 us
    all_to_all x1, waiting for transfers between devices, per_device_body(): lax.all_to_all(value_payload, 'seq', split_axis=0, concat_axis=0, tiled=T...  78.7 us
    all_to_all x1, blocking collectives, per_device_body(): lax.all_to_all(group, 'seq', split_axis=0, concat_axis=0, tiled=True)  53.9 us
    unnamed x60, local copies, waits for them, and re-layouts  38.7 us
    all_to_all x3, starting transfers between devices, per_device_body(): lax.all_to_all(payload, 'seq', split_axis=0, concat_axis=0, tiled=True)  16.4 us
    concatenate x3, other arithmetic, per_device_body(): jnp.concatenate([by_destination(array, heads) for array in normed], axis=1)  10 us
  transfers between devices with their start and end apart: 5, of which 4 were waited for; matrix products, arithmetic and copies ran while one was open for 5% of the time, Pallas kernels for 23%

commit v1 on v0

--- a/solution.py
+++ b/solution.py
@@ -220,12 +220,7 @@
     )(*received)
 
 
-def chunk_sizes(local_heads):
-    if local_heads <= 2:
-        return [1] * local_heads
-    return [1, 1, local_heads - 2]
-
-
+CHUNKS = 4
 RESULT_DTYPE = jnp.bfloat16
 
 
@@ -237,8 +232,8 @@
     width = q_proj.shape[2]
     local_heads = width // HEAD_DIM // seq_count
     pack_tokens = tokens * seq_count
-    sizes = chunk_sizes(local_heads)
-    starts = [sum(sizes[:c]) for c in range(len(sizes))]
+    chunks = min(CHUNKS, local_heads)
+    chunk_heads = local_heads // chunks
 
     assert tokens == BLOCK
 
@@ -251,24 +246,23 @@
 
     q_normed, dq_normed = normalize(q_proj, q_tangent, query_norm_gain)
     k_normed, dk_normed = normalize(k_proj, k_tangent, key_norm_gain)
-    own_row = lax.dynamic_slice_in_dim(lengths, lax.axis_index("samp"), 1, 0)[0]
+    shared = lax.ppermute(lengths, "seq", [(s, (s + 1) % seq_count) for s in range(seq_count)])
+    own_row = lax.dynamic_slice_in_dim(shared, lax.axis_index("samp"), 1, 0)[0]
     first_block, last_block, sample_ends = block_tables(own_row, pack_tokens)
     normed = (q_normed, dq_normed, k_normed, dk_normed)
     results = []
-    for first_head, chunk_heads in zip(starts, sizes):
-        heads = slice(first_head, first_head + chunk_heads)
+    for c in range(chunks):
+        heads = slice(c * chunk_heads, (c + 1) * chunk_heads)
         payload = jnp.concatenate([by_destination(array, heads) for array in normed], axis=1)
         stacked = lax.all_to_all(payload, "seq", split_axis=0, concat_axis=0, tiled=True)
         result = attend(
-            stacked, values, chunk_heads, first_head,
+            stacked, values, chunk_heads, c * chunk_heads,
             first_block, last_block, sample_ends, RESULT_DTYPE,
         )
         results.append(result)
     received = []
-    for members in (results[:2], results[2:]):
-        if not members:
-            continue
-        group = jnp.concatenate(members, axis=3)
+    for g in range(0, chunks, 2):
+        group = jnp.concatenate(results[g:g + 2], axis=3)
         received.append(lax.all_to_all(group, "seq", split_axis=0, concat_axis=0, tiled=True))
     return tuple(assemble(received, tokens, width))
 

time: 458 us -> 528 us (1.15)
  waiting for transfers between devices: 198 us -> 249 us
  starting transfers between devices: 24.6 us -> 37.5 us
    ppermute x0 -> x1, waiting for transfers between devices: none -> 37.1 us  [per_device_body(): lax.ppermute(lengths, 'seq', [(s, (s + 1) % seq_count) for s in range(seq...]
    all_to_all x1, waiting for transfers between devices: 78.7 us -> 89.4 us  [per_device_body(): lax.all_to_all(value_payload, 'seq', split_axis=0, concat_axis=0, tiled=T...]
    all_to_all x1, starting transfers between devices: 3.61 us -> 12 us  [per_device_body(): lax.all_to_all(group, 'seq', split_axis=0, concat_axis=0, tiled=True)]
    all_to_all x3 -> x4, waiting for transfers between devices: 119 us -> 123 us  [per_device_body(): lax.all_to_all(payload, 'seq', split_axis=0, concat_axis=0, tiled=True)]
    all_to_all x3 -> x4, starting transfers between devices: 16.4 us -> 18.9 us  [per_device_body(): lax.all_to_all(payload, 'seq', split_axis=0, concat_axis=0, tiled=True)]
    pallas_call x3 -> x4, Pallas kernels: 103 us -> 105 us  [attend(): pl.pallas_call(attention_kernel, grid_spec=grid_spec, out_shape=jax.Shape...]
    unnamed x60 -> x54, local copies, waits for them, and re-layouts: 38.7 us -> 39 us
  transfers between devices with their start and end apart: 5 -> 7, of which waited for: 4 -> 5; matrix products, arithmetic and copies ran while one was open for 5% -> 5% of each run, Pallas kernels for 23% -> 21%
where the time goes in v1:
time: 528 us; the launch traced here: 526 us
  waiting for transfers between devices  249 us (47%)
  Pallas kernels  114 us (22%)
  blocking collectives  53.6 us (10%)
  local copies, waits for them, and re-layouts  45.4 us (9%)
  starting transfers between devices  37.5 us (7%)
  other arithmetic  25.6 us (5%)
    all_to_all x4, waiting for transfers between devices, per_device_body(): lax.all_to_all(payload, 'seq', split_axis=0, concat_axis=0, tiled=True)  123 us
    pallas_call x4, Pallas kernels, attend(): pl.pallas_call(attention_kernel, grid_spec=grid_spec, out_shape=jax.Shape...  105 us
    all_to_all x1, waiting for transfers between devices, per_device_body(): lax.all_to_all(value_payload, 'seq', split_axis=0, concat_axis=0, tiled=T...  89.4 us
    all_to_all x1, blocking collectives, per_device_body(): lax.all_to_all(group, 'seq', split_axis=0, concat_axis=0, tiled=True)  53.6 us
    unnamed x54, local copies, waits for them, and re-layouts  39 us
    ppermute x1, waiting for transfers between devices, per_device_body(): lax.ppermute(lengths, 'seq', [(s, (s + 1) % seq_count) for s in range(seq...  37.1 us
    all_to_all x4, starting transfers between devices, per_device_body(): lax.all_to_all(payload, 'seq', split_axis=0, concat_axis=0, tiled=True)  18.9 us
    all_to_all x1, starting transfers between devices, per_device_body(): lax.all_to_all(group, 'seq', split_axis=0, concat_axis=0, tiled=True)  12 us
  transfers between devices with their start and end apart: 7, of which 5 were waited for; matrix products, arithmetic and copies ran while one was open for 5% of the time, Pallas kernels for 21%

profile of v1, /device:TPU:0, one launch (start us, length us, event | category | flops | bytes accessed | tf_op | source)
XLA Modules:
  0.0 526.1 jit_solution(835982742391604169)
XLA Ops:
  0.6 3.3 copy.31
  3.9 4.1 copy.33
  8.0 2.6 fusion.6
  10.7 2.4 fusion.8
  18.5 3.3 copy.35
  21.7 4.1 copy.37
  25.8 2.6 fusion.11
  28.5 2.4 fusion.13
  32.2 2.1 copy.62
  37.0 2.9 pad_maximum_fusion.3
  40.0 7.3 %all-to-all-start.4 = ((bf16[8,4,256,128]{3,2,1,0:T(8,128)(2,1)}), bf16[8,4,256,128]{3,2,1,0:T(8,128)(2,1)S(1)}, u32[]{:S(2)}, u32[]{:S(2)}) async-start(bf16[8,4,256,128]{3,2,1,0:T(8,128)(2,1)} %pad_maximum_fusion.3), calls=%async_computation.4 | async-start | bytes 4194304 | tf_op jit(solution)/shard_map/all_to_all | solution.py:257
  53.4 2.1 copy.58
  55.5 3.1 pad_maximum_fusion.1
  58.5 37.0 %all-to-all-done.4.q_ref.dq_ref.k_ref.dk_ref = bf16[8,4,256,128]{3,2,1,0:T(8,128)(2,1)S(1)} async-done(((bf16[8,4,256,128]{3,2,1,0:T(8,128)(2,1)}), bf16[8,4,256,128]{3,2,1,0:T(8,128)(2,1)S(1)}, u32[]{:S(2)}, u32[]{:S(2)}) %all-to-all-start.4) | async-done | bytes 2097184 | tf_op jit(solution)/shard_map/all_to_all | solution.py:257
  96.9 4.4 all-to-all-start.2
  105.3 2.6 pad_maximum_fusion.4
  108.0 41.1 %all-to-all-done.2.q_ref.dq_ref.k_ref.dk_ref = bf16[8,4,256,128]{3,2,1,0:T(8,128)(2,1)} async-done(((bf16[8,4,256,128]{3,2,1,0:T(8,128)(2,1)}), bf16[8,4,256,128]{3,2,1,0:T(8,128)(2,1)}, u32[]{:S(2)}, u32[]{:S(2)}) %all-to-all-start.2) | async-done | bytes 2097184 | tf_op jit(solution)/shard_map/all_to_all | solution.py:257
  149.0 3.6 all-to-all-start.5
  152.7 3.9 shard_map.104
  156.6 44.5 %all-to-all-done.5.q_ref.dq_ref.k_ref.dk_ref = bf16[8,4,256,128]{3,2,1,0:T(8,128)(2,1)S(1)} async-done(((bf16[8,4,256,128]{3,2,1,0:T(8,128)(2,1)}), bf16[8,4,256,128]{3,2,1,0:T(8,128)(2,1)S(1)}, u32[]{:S(2)}, u32[]{:S(2)}) %all-to-all-start.5) | async-done | bytes 2097184 | tf_op jit(solution)/shard_map/all_to_all | solution.py:257
  202.5 4.6 all-to-all-start.1
  210.2 89.4 %all-to-all-done.1.v_ref.dv_ref = bf16[8,8,256,128]{3,2,1,0:T(8,128)(2,1)} async-done(((bf16[8,8,256,128]{3,2,1,0:T(8,128)(2,1)}), bf16[8,8,256,128]{3,2,1,0:T(8,128)(2,1)}, u32[]{:S(2)}, u32[]{:S(2)}) %all-to-all-start.1) | async-done | bytes 4194336 | tf_op jit(solution)/shard_map/all_to_all | solution.py:245
  299.6 3.6 all-to-all-start
  305.3 37.1 %collective-permute-done = s32[2,4]{1,0:T(2,128)S(1)} collective-permute-done((s32[2,4]{1,0:T(2,128)S(1)}, s32[2,4]{1,0:T(2,128)S(1)}, u32[]{:S(2)}, u32[]{:S(2)}) %collective-permute-start) | collective-permute-done | bytes 64 | tf_op jit(solution)/shard_map/ppermute | solution.py:249
  344.6 26.2 %shard_map.108 = bf16[8,2,256,128]{3,2,1,0:T(8,128)(2,1)} custom-call(s32[8]{0:T(128)} %get-tuple-element.10.first_ref, s32[8]{0:T(128)} %get-tuple-element.9.last_ref, s32[4]{0:T(128)} %bitcast.28, bf16[8,4,256,128]{3,2,1,0:T(8,128)(2,1)} %copy-done.2, bf16[8,4,256,128]{3,2,1,0:T(8,128)(2,1)} %copy-done.2, bf16[8,4,256,128]{3,2,1,0:T(8,128)(2,1)} %copy-done.2, ...), custom_call_target="tpu_custom_call" | custom-call | tf_op jit(solution)/shard_map/pallas_call | solution.py:142
  370.8 26.3 %shard_map.107 = bf16[8,2,256,128]{3,2,1,0:T(8,128)(2,1)} custom-call(s32[8]{0:T(128)} %get-tuple-element.10.first_ref, s32[8]{0:T(128)} %get-tuple-element.9.last_ref, s32[4]{0:T(128)} %bitcast.29, bf16[8,4,256,128]{3,2,1,0:T(8,128)(2,1)} %copy-done.1, bf16[8,4,256,128]{3,2,1,0:T(8,128)(2,1)} %copy-done.1, bf16[8,4,256,128]{3,2,1,0:T(8,128)(2,1)} %copy-done.1, ...), custom_call_target="tpu_custom_call" | custom-call | tf_op jit(solution)/shard_map/pallas_call | solution.py:142
  397.1 2.9 pad_maximum_fusion.5
  401.3 12.0 %all-to-all-start.6 = ((bf16[8,2,256,256]{3,2,1,0:T(8,128)(2,1)}), bf16[8,2,256,256]{3,2,1,0:T(8,128)(2,1)}, u32[]{:S(2)}, u32[]{:S(2)}) async-start(bf16[8,2,256,256]{3,2,1,0:T(8,128)(2,1)} %pad_maximum_fusion.5), calls=%async_computation.6 | async-start | bytes 4194304 | tf_op jit(solution)/shard_map/all_to_all | solution.py:266
  413.4 26.2 %shard_map.106 = bf16[8,2,256,128]{3,2,1,0:T(8,128)(2,1)} custom-call(s32[8]{0:T(128)} %get-tuple-element.10.first_ref, s32[8]{0:T(128)} %get-tuple-element.9.last_ref, s32[4]{0:T(128)} %bitcast.30, bf16[8,4,256,128]{3,2,1,0:T(8,128)(2,1)} %all-to-all-done.2.q_ref.dq_ref.k_ref.dk_ref, bf16[8,4,256,128]{3,2,1,0:T(8,128)(2,1)} %all-to-all-done.2.q_ref.dq_ref.k_ref.dk_ref, ...), custom_call_target="tpu_custom_call" | custom-call | tf_op jit(solution)/shard_map/pallas_call | solution.py:142
  439.5 26.3 %shard_map.105 = bf16[8,2,256,128]{3,2,1,0:T(8,128)(2,1)} custom-call(s32[8]{0:T(128)} %get-tuple-element.10.first_ref, s32[8]{0:T(128)} %get-tuple-element.9.last_ref, s32[4]{0:T(128)} %bitcast.31, bf16[8,4,256,128]{3,2,1,0:T(8,128)(2,1)} %copy-done.3, bf16[8,4,256,128]{3,2,1,0:T(8,128)(2,1)} %copy-done.3, bf16[8,4,256,128]{3,2,1,0:T(8,128)(2,1)} %copy-done.3, ...), custom_call_target="tpu_custom_call" | custom-call | tf_op jit(solution)/shard_map/pallas_call | solution.py:142
  467.4 53.6 %all_to_all.35.refs_0_ = bf16[8,2,256,256]{3,2,1,0:T(8,128)(2,1)} all-to-all(bf16[8,2,256,256]{3,2,1,0:T(8,128)(2,1)S(1)} %pad_maximum_fusion.2), channel_id=1, replica_groups=mesh['groups'=2,'seq'=8,'samp'=2] {'seq'}, dimensions={0} | all-to-all | bytes 4194304 | tf_op jit(solution)/shard_map/all_to_all | solution.py:266
  521.0 5.1 shard_map.109
  (71 shorter events, 32.6 us)
Async XLA Ops:
  8.0 2.6 copy-start.4
  8.0 2.7 copy-start.14
  13.1 2.1 copy-start.6
  25.8 2.6 copy-start.5
  25.8 2.7 copy-start.15
  30.9 3.4 copy-start.7
  40.0 55.5 %all-to-all-start.4 = ((bf16[8,4,256,128]{3,2,1,0:T(8,128)(2,1)}), bf16[8,4,256,128]{3,2,1,0:T(8,128)(2,1)S(1)}, u32[]{:S(2)}, u32[]{:S(2)}) async-start(bf16[8,4,256,128]{3,2,1,0:T(8,128)(2,1)} %pad_maximum_fusion.3), calls=%async_computation.4 | async-start | bytes 4194304 | tf_op jit(solution)/shard_map/all_to_all | solution.py:257
  95.5 1.4 copy-start.1
  96.9 52.2 %all-to-all-start.2 = ((bf16[8,4,256,128]{3,2,1,0:T(8,128)(2,1)}), bf16[8,4,256,128]{3,2,1,0:T(8,128)(2,1)}, u32[]{:S(2)}, u32[]{:S(2)}) async-start(bf16[8,4,256,128]{3,2,1,0:T(8,128)(2,1)} %pad_maximum_fusion.1), calls=%async_computation.2 | async-start | bytes 4194304 | tf_op jit(solution)/shard_map/all_to_all | solution.py:257
  101.2 2.7 copy-start.13
  101.3 3.8 copy-start.12
  149.0 52.0 %all-to-all-start.5 = ((bf16[8,4,256,128]{3,2,1,0:T(8,128)(2,1)}), bf16[8,4,256,128]{3,2,1,0:T(8,128)(2,1)S(1)}, u32[]{:S(2)}, u32[]{:S(2)}) async-start(bf16[8,4,256,128]{3,2,1,0:T(8,128)(2,1)} %pad_maximum_fusion.4), calls=%async_computation.5 | async-start | bytes 4194304 | tf_op jit(solution)/shard_map/all_to_all | solution.py:257
  201.1 1.4 copy-start.2
  202.5 97.1 %all-to-all-start.1 = ((bf16[8,8,256,128]{3,2,1,0:T(8,128)(2,1)}), bf16[8,8,256,128]{3,2,1,0:T(8,128)(2,1)}, u32[]{:S(2)}, u32[]{:S(2)}) async-start(bf16[8,8,256,128]{3,2,1,0:T(8,128)(2,1)} %shard_map.104), calls=%async_computation.1 | async-start | bytes 8388608 | tf_op jit(solution)/shard_map/all_to_all | solution.py:245
  207.1 1.0 copy-start.11
  207.1 1.3 copy-start.10
  210.2 93.0 %copy-start.16 = (s32[2,4]{1,0:T(2,128)S(1)}, s32[2,4]{1,0:T(2,128)}, u32[]{:S(2)}) copy-start(s32[2,4]{1,0:T(2,128)} %param.19) | copy-start | bytes 100
  299.6 100.4 %all-to-all-start = ((bf16[8,4,256,128]{3,2,1,0:T(8,128)(2,1)}), bf16[8,4,256,128]{3,2,1,0:T(8,128)(2,1)S(1)}, u32[]{:S(2)}, u32[]{:S(2)}) async-start(bf16[8,4,256,128]{3,2,1,0:T(8,128)(2,1)} %pad_maximum_fusion), calls=%async_computation | async-start | bytes 4194304 | tf_op jit(solution)/shard_map/all_to_all | solution.py:257
  303.2 39.1 %collective-permute-start = (s32[2,4]{1,0:T(2,128)S(1)}, s32[2,4]{1,0:T(2,128)S(1)}, u32[]{:S(2)}, u32[]{:S(2)}) collective-permute-start(s32[2,4]{1,0:T(2,128)S(1)} %copy-done.16), channel_id=1, source_target_pairs={{0,2},{2,4},{4,6},{6,8},{8,10},{10,12},{12,14},{14,0},{1,3},{3,5},... | collective-permute-start | bytes 104 | tf_op jit(solution)/shard_map/ppermute | solution.py:249
  342.6 2.0 copy-start
  370.8 26.3 %copy-start.9 = (bf16[8,2,256,128]{3,2,1,0:T(8,128)(2,1)S(1)}, bf16[8,2,256,128]{3,2,1,0:T(8,128)(2,1)}, u32[]{:S(2)}) copy-start(bf16[8,2,256,128]{3,2,1,0:T(8,128)(2,1)} %shard_map.108) | copy-start | bytes 3145732
  400.0 1.3 copy-start.3
  401.3 66.1 %all-to-all-start.6 = ((bf16[8,2,256,256]{3,2,1,0:T(8,128)(2,1)}), bf16[8,2,256,256]{3,2,1,0:T(8,128)(2,1)}, u32[]{:S(2)}, u32[]{:S(2)}) async-start(bf16[8,2,256,256]{3,2,1,0:T(8,128)(2,1)} %pad_maximum_fusion.5), calls=%async_computation.6 | async-start | bytes 4194304 | tf_op jit(solution)/shard_map/all_to_all | solution.py:266
  439.5 26.3 %copy-start.8 = (bf16[8,2,256,128]{3,2,1,0:T(8,128)(2,1)S(1)}, bf16[8,2,256,128]{3,2,1,0:T(8,128)(2,1)}, u32[]{:S(2)}) copy-start(bf16[8,2,256,128]{3,2,1,0:T(8,128)(2,1)} %shard_map.106) | copy-start | bytes 3145732
